TPU v7x, 512 devices: a whole 4x4x16 slice. The times are simulated.
512 devices in a mesh: grp: 4 (over x), ch: 128 (over y, z, core).
Axes of the slice: x: 4, y: 4, z: 16, core: 2. Of those that a mesh axis runs over, the one named last changes fastest.
Arguments:
- raw_strain: bfloat16 [4, 7680, 8192], P('grp', 'ch'), may hold values from -6 to 6
- window_valid: int32 [4, 8192], P(None, 'ch'), may hold values 0 or 1
- band_first: int32 [8192], P('ch'), may hold values from 1 to 17
- band_end: int32 [8192], P('ch'), may hold values from 34 to 128
Outputs:
- stacked: float32 [8192, 32, 128], P('ch')
All inputs are finite; a program needn't handle non-finite values. No bound on the sum of `window_valid` on one device may be relied on, other than what follows from the above.
Results may differ from a plain program's by a relative error of at most 0.008.
Values may be sent and summed in bfloat16 or wider, within the bound.
No kernel may reach another device: no remote copies, remote signals or barrier semaphores. Data moves between devices by JAX's collectives and lax.ppermute only.
A program may use at most 64 MiB of HBM per device.

v0:
```python
import jax
import jax.numpy as jnp
from jax import lax
from jax.sharding import PartitionSpec as P

NT = 7680
F = 384
KH = 128
SMOOTH = 65
LAGS = 32
LAG_STEP = 10


eps_white = 1e-06


def from_behind(array, axis, by):
    count = lax.axis_size(axis)
    pairs = [(i, i + by) for i in range(count) if 0 <= i + by < count]
    return lax.ppermute(array, axis, pairs)


def dft_matrix(samples, bin_count):
    sample_index = jnp.arange(samples, dtype=jnp.int32)[:, None]
    orders = jnp.arange(1, bin_count + 1, dtype=jnp.int32)[None, :]
    phases = (sample_index * orders % samples).astype(jnp.float32) * (2.0 * jnp.pi / samples)
    return jnp.concatenate([jnp.cos(phases), -jnp.sin(phases)], axis=1).astype(jnp.bfloat16)


def smoothing_matrix(bin_count, window_bins):
    row_index = jnp.arange(bin_count, dtype=jnp.int32)[:, None]
    col_index = jnp.arange(bin_count, dtype=jnp.int32)[None, :]
    distance = (row_index - col_index) % bin_count
    halfwidth = window_bins // 2
    inside = (distance <= halfwidth) | (distance >= bin_count - halfwidth)
    return inside.astype(jnp.float32)


def whiten(spectra, bin_count, window_bins):
    real_part = spectra[..., :bin_count]
    imag_part = spectra[..., bin_count:]
    magnitude = jnp.sqrt(real_part * real_part + imag_part * imag_part)
    averaged = (
        jnp.dot(
            magnitude,
            smoothing_matrix(bin_count, window_bins),
            precision=lax.Precision.HIGHEST,
            preferred_element_type=jnp.float32,
        )
        / window_bins
    )
    factor = 1.0 / (averaged + eps_white)
    return (spectra * jnp.concatenate([factor, factor], axis=-1)).astype(jnp.bfloat16)


def rotated(extended, lag_first, lag_count, lag_step, samples, bin_count):
    orders = jnp.arange(1, bin_count + 1, dtype=jnp.int32)[None, :]
    shifts = ((lag_first + jnp.arange(lag_count, dtype=jnp.int32)) * lag_step)[:, None]
    phases = (shifts * orders % samples).astype(jnp.float32) * (2.0 * jnp.pi / samples)
    cosine = jnp.cos(phases)
    sine_part = jnp.sin(phases)
    real_part = extended[..., :bin_count].astype(jnp.float32)[:, :, None, :]
    imag_part = extended[..., bin_count:].astype(jnp.float32)[:, :, None, :]
    rotated_real = real_part * cosine + imag_part * sine_part
    rotated_imag = imag_part * cosine - real_part * sine_part
    return jnp.concatenate([rotated_real, rotated_imag], axis=-1).astype(jnp.bfloat16)


def diagonal_band(matrix, offsets):
    row_count, col_count = matrix.shape
    flat_rows = matrix.reshape(row_count * col_count)
    padded = jnp.concatenate([flat_rows, jnp.zeros((row_count,), matrix.dtype)])
    skewed = padded.reshape(row_count, col_count + 1)
    return skewed[:, :offsets]


def lag_band(block_full, offsets):
    banded = jax.vmap(lambda matrix: diagonal_band(matrix, offsets))(block_full)
    return jnp.transpose(banded, (1, 0, 2))


def normalise(lagged, pair_counts, band_lows, band_highs, bin_count):
    offsets = jnp.arange(lagged.shape[2], dtype=jnp.int32)[None, :]
    in_band = (offsets >= band_lows[:, None]) & (offsets < band_highs[:, None])
    weights = jnp.where(
        in_band, 1.0 / jnp.sqrt(float(bin_count) * jnp.maximum(pair_counts, 1.0)), 0.0
    )
    return lagged * weights[:, None, :]


def local(raw_strain, window_valid, band_first, band_end):
    dft_table = dft_matrix(NT, F)
    spectra = jnp.einsum(
        "nta,tf->naf",
        lax.all_to_all(raw_strain, "ch", split_axis=2, concat_axis=1, tiled=True),
        dft_table,
        preferred_element_type=jnp.float32,
    )
    whitened = whiten(spectra, F, SMOOTH)
    valid_flags = window_valid.astype(jnp.bfloat16)
    group_index = lax.axis_index("grp")
    own_flags = lax.dynamic_slice_in_dim(valid_flags, group_index, 1, 0)
    whitened = whitened * own_flags[:, :, None]
    channels_here = whitened.shape[1]
    blocks_up = (KH + channels_here - 1) // channels_here
    white_parts = [whitened]
    flag_parts = [valid_flags]
    for neighbour in range(1, blocks_up + 1):
        moved_white, moved_flags = from_behind((whitened, valid_flags), "ch", -neighbour)
        white_parts.append(moved_white)
        flag_parts.append(moved_flags)
    extended = jnp.concatenate(white_parts, axis=1)
    ext_flags = jnp.concatenate(flag_parts, axis=1)
    pair_full = jnp.einsum("na,nb->ab", valid_flags, ext_flags, preferred_element_type=jnp.float32)
    pair_counts = diagonal_band(pair_full, KH)
    turned = rotated(extended, -(LAGS // 2), LAGS, LAG_STEP, NT, F)
    block_full = jnp.einsum("nak,nblk->lab", whitened, turned, preferred_element_type=jnp.float32)
    lagged = lax.psum(lag_band(block_full, KH).astype(jnp.bfloat16), "grp").astype(jnp.float32)
    return normalise(lagged, pair_counts, band_first, band_end, F)


def solution(mesh):
    placed = (P("grp", "ch", None), P(None, "ch"), P("ch"), P("ch"))
    return jax.shard_map(
        local, mesh=mesh, in_specs=placed, out_specs=P("ch", None, None), check_vma=False
    )
```

profile of v0, /device:TPU:16, one launch (start us, length us, event | category | flops | bytes accessed | tf_op | source)
XLA Modules:
  0.0 264.3 jit_solution(14576265745442213151)
XLA Ops:
  6.5 9.2 %copy.8 = bf16[1,60,8192]{1,0,2:T(2,128)(2,1)} copy(bf16[1,60,8192]{2,1,0:T(8,128)(2,1)} %param.4) | data formatting | bytes 1966080 | tf_op args[0]
  15.7 0.0 copy-start
  15.7 0.5 broadcast.138
  16.3 45.2 %reduce = bf16[8192,60]{1,0:T(8,128)(2,1)S(1)} reduce(bf16[8192,1,60]{2,1,0:T(2,128)(2,1)} %bitcast.40, bf16[]{:T(256)} %broadcast.138), dimensions={1}, to_apply=%bitcast.36.reduce_sub_computation | reduce | bytes 1966082
  61.5 6.4 %reshape.150 = bf16[128,2,1920]{2,1,0:T(2,128)(2,1)} reshape(bf16[8192,60]{1,0:T(8,128)(2,1)S(1)} %reduce) | data formatting | bytes 1966080
  67.9 19.7 %all-to-all-start = ((bf16[128,2,1920]{2,1,0:T(2,128)(2,1)}), bf16[128,2,1920]{2,1,0:T(2,128)(2,1)S(1)}, u32[]{:S(2)}, u32[]{:S(2)}) async-start(bf16[128,2,1920]{2,1,0:T(2,128)(2,1)} %reshape.150), calls=%async_computation | async-start | bytes 1966080 | tf_op jit(solution)/shard_map/all_to_all | solution.py:95
  87.6 0.2 all-reduce.4.cloned.1.call-start
  87.8 0.0 copy-done
  87.9 50.6 %cosine_convert_fusion = (bf16[7680,384]{1,0:T(8,128)(2,1)}, bf16[7680,384]{1,0:T(8,128)(2,1)}) fusion(s32[384]{0:T(512)S(1)} %iota_add_fusion), kind=kLoop, calls=%fused_computation.8 | loop fusion | flops 35389440 | bytes 11798016 | tf_op jit(solution)/shard_map/convert.10
  138.5 1.7 all-to-all-done
  140.2 9.5 %reshape.151 = bf16[8192,1,60]{2,1,0:T(2,128)(2,1)} reshape(bf16[128,2,1920]{2,1,0:T(2,128)(2,1)S(1)} %all-to-all-done) | data formatting | bytes 1966080
  149.7 8.4 %copy.9 = bf16[1,60,8192]{2,1,0:T(8,128)(2,1)S(1)} copy(bf16[1,60,8192]{1,0,2:T(2,128)(2,1)} %bitcast.41) | data formatting | bytes 1966080 | tf_op jit(solution)/shard_map/all_to_all | solution.py:95
  158.1 3.5 %all_to_all.12 = bf16[1,60,128,64]{3,2,1,0:T(8,128)(2,1)} reshape(bf16[1,60,8192]{2,1,0:T(8,128)(2,1)S(1)} %copy.9) | data formatting | bytes 1966080 | tf_op jit(solution)/shard_map/all_to_all | solution.py:95
  161.6 4.7 %copy.10 = bf16[1,128,60,64]{2,1,3,0:T(8,128)(2,1)S(1)} copy(bf16[1,128,60,64]{3,1,2,0:T(8,128)(2,1)} %bitcast.42) | data formatting | bytes 1966080 | tf_op jit(solution)/shard_map/all_to_all | solution.py:95
  166.3 4.1 %reshape.141 = bf16[7680,64]{0,1:T(8,128)(2,1)S(1)} reshape(bf16[1,128,60,64]{2,1,3,0:T(8,128)(2,1)S(1)} %copy.10) | data formatting | bytes 1966080 | tf_op jit(solution)/shard_map/reshape
  170.4 5.6 %fusion.2 = f32[768,64]{0,1:T(8,128)S(1)} fusion(bf16[7680,64]{0,1:T(8,128)(2,1)S(1)} %reshape.141, bf16[7680,384]{1,0:T(8,128)(2,1)} %get-tuple-element.12, bf16[7680,384]{1,0:T(8,128)(2,1)} %get-tuple-element.11), kind=kOutput, calls=%fused_computation.3 | convolution fusion | flops 778567680 | bytes 12976128 | tf_op jit(solution)/shard_map/nta,tf->naf/dot_general | solution.py:93
  176.0 0.7 fusion.20
  176.7 0.1 fusion.35
  176.8 2.9 %collective-permute-start.1 = (bf16[1,64,768]{2,1,0:T(8,128)(2,1)S(1)}, bf16[1,64,768]{2,1,0:T(8,128)(2,1)S(1)}, u32[]{:S(2)}, u32[]{:S(2)}) collective-permute-start(bf16[1,64,768]{2,1,0:T(8,128)(2,1)S(1)} %bitcast.43), channel_id=1, source_target_pairs={{2,0},{3,1},{4,2},{5,3},{6,4},{7,5},{8,6},{9,7},{10,8},{11,9},{12,... | collective-permute-start | bytes 294920 | tf_op jit(solution)/shard_map/ppermute | solution.py:20
  179.6 3.0 %collective-permute-start = (bf16[1,64,768]{2,1,0:T(8,128)(2,1)S(1)}, bf16[1,64,768]{2,1,0:T(8,128)(2,1)S(1)}, u32[]{:S(2)}, u32[]{:S(2)}) collective-permute-start(bf16[1,64,768]{2,1,0:T(8,128)(2,1)S(1)} %bitcast.44), channel_id=1, source_target_pairs={{1,0},{2,1},{3,2},{4,3},{5,4},{6,5},{7,6},{8,7},{9,8},{10,9},{11,1... | collective-permute-start | bytes 294920 | tf_op jit(solution)/shard_map/ppermute | solution.py:20
  182.7 0.3 fusion.46
  183.0 0.3 collective-permute-done.1
  183.3 1.4 collective-permute-done
  184.7 2.6 add_convert_fusion
  187.3 2.9 %fusion.16 = bf16[32,64,192]{1,0,2:T(8,128)(2,1)S(1)} fusion(bf16[192,32,384]{2,1,0:T(8,128)(2,1)S(1)} %get-tuple-element.6, bf16[192,32,384]{2,1,0:T(8,128)(2,1)S(1)} %get-tuple-element.5, bf16[64,768]{1,0:T(8,128)(2,1)S(1)} %fusion.35), kind=kOutput, calls=%fused_computation.20 | convolution fusion | flops 623247360 | bytes 10321920 | tf_op jit(solution)/shard_map/nak,nblk->lab/dot_general | solution.py:117
  190.3 0.0 copy-start.1
  190.3 0.0 copy-start.2
  190.3 1.4 copy.11
  191.7 1.1 reshape.143
  192.8 0.1 concatenate.31
  192.9 3.2 %reshape.144 = bf16[32,64,193]{2,1,0:T(8,128)(2,1)S(1)} reshape(bf16[32,12352]{1,0:T(8,128)(2,1)S(1)} %concatenate.31) | data formatting | bytes 1581056 | tf_op jit(solution)/shard_map/vmap()/reshape | solution.py:73
  196.1 0.9 slice_bitcast_fusion
  197.0 0.0 all-reduce.4.cloned.1.call-update
  197.0 3.8 %collective-permute-start.3 = (bf16[4,64]{1,0:T(4,128)(2,1)S(1)}, bf16[4,64]{1,0:T(4,128)(2,1)S(1)}, u32[]{:S(2)}, u32[]{:S(2)}) collective-permute-start(bf16[4,64]{1,0:T(4,128)(2,1)S(1)} %convert_element_type.45), channel_id=1, source_target_pairs={{2,0},{3,1},{4,2},{5,3},{6,4},{7,5},{8,6},{9,7},{10,8},{11,9},{12,... | collective-permute-start | bytes 1544 | tf_op jit(solution)/shard_map/ppermute | solution.py:20
  200.8 4.0 %collective-permute-start.2 = (bf16[4,64]{1,0:T(4,128)(2,1)S(1)}, bf16[4,64]{1,0:T(4,128)(2,1)S(1)}, u32[]{:S(2)}, u32[]{:S(2)}) collective-permute-start(bf16[4,64]{1,0:T(4,128)(2,1)S(1)} %convert_element_type.45), channel_id=1, source_target_pairs={{1,0},{2,1},{3,2},{4,3},{5,4},{6,5},{7,6},{8,7},{9,8},{10,9},{11,1... | collective-permute-start | bytes 1544 | tf_op jit(solution)/shard_map/ppermute | solution.py:20
  204.8 0.0 collective-permute-done.3
  204.8 1.3 collective-permute-done.2
  206.0 0.2 convolution_bitcast_fusion
  206.2 0.1 reshape.145
  206.4 0.2 reshape.146
  206.6 0.0 copy-done.1
  206.6 0.0 copy-done.2
  206.6 0.1 fusion.50
  206.7 48.0 %all-reduce.4.cloned.1.call-done = bf16[64,32,128]{2,0,1:T(8,128)(2,1)} async-done(((bf16[64,32,128]{2,0,1:T(8,128)(2,1)}), bf16[64,32,128]{2,0,1:T(8,128)(2,1)}) %all-reduce.4.cloned.1.call-update) | async-done | bytes 524304 | tf_op jit(solution)/shard_map/psum | solution.py:118
  254.7 1.2 convert_multiply_fusion
  255.9 1.6 copy.12
  (7 shorter events, 0.1 us)
Async XLA Ops:
  15.7 72.1 %copy-start = (s32[4,64]{1,0:T(4,128)S(1)}, s32[4,64]{1,0:T(4,128)}, u32[]{:S(2)}) copy-start(s32[4,64]{1,0:T(4,128)} %param.5) | copy-start | bytes 3076
  67.9 72.3 %all-to-all-start = ((bf16[128,2,1920]{2,1,0:T(2,128)(2,1)}), bf16[128,2,1920]{2,1,0:T(2,128)(2,1)S(1)}, u32[]{:S(2)}, u32[]{:S(2)}) async-start(bf16[128,2,1920]{2,1,0:T(2,128)(2,1)} %reshape.150), calls=%async_computation | async-start | bytes 1966080 | tf_op jit(solution)/shard_map/all_to_all | solution.py:95
  87.6 167.1 %all-reduce.4.cloned.1.call-start = ((), (), s32[]{:S(2)}) async-start(), calls=%async_computation.1 | async-start | bytes 1048576 | tf_op jit(solution)/shard_map/psum | solution.py:118
  176.8 6.5 %collective-permute-start.1 = (bf16[1,64,768]{2,1,0:T(8,128)(2,1)S(1)}, bf16[1,64,768]{2,1,0:T(8,128)(2,1)S(1)}, u32[]{:S(2)}, u32[]{:S(2)}) collective-permute-start(bf16[1,64,768]{2,1,0:T(8,128)(2,1)S(1)} %bitcast.43), channel_id=1, source_target_pairs={{2,0},{3,1},{4,2},{5,3},{6,4},{7,5},{8,6},{9,7},{10,8},{11,9},{12,... | collective-permute-start | bytes 294920 | tf_op jit(solution)/shard_map/ppermute | solution.py:20
  179.6 5.0 %collective-permute-start = (bf16[1,64,768]{2,1,0:T(8,128)(2,1)S(1)}, bf16[1,64,768]{2,1,0:T(8,128)(2,1)S(1)}, u32[]{:S(2)}, u32[]{:S(2)}) collective-permute-start(bf16[1,64,768]{2,1,0:T(8,128)(2,1)S(1)} %bitcast.44), channel_id=1, source_target_pairs={{1,0},{2,1},{3,2},{4,3},{5,4},{6,5},{7,6},{8,7},{9,8},{10,9},{11,1... | collective-permute-start | bytes 294920 | tf_op jit(solution)/shard_map/ppermute | solution.py:20
  190.3 16.3 %copy-start.1 = (s32[64]{0:T(128)S(1)}, s32[64]{0:T(128)}, u32[]{:S(2)}) copy-start(s32[64]{0:T(128)} %param.7) | copy-start | bytes 772
  190.3 16.3 %copy-start.2 = (s32[64]{0:T(128)S(1)}, s32[64]{0:T(128)}, u32[]{:S(2)}) copy-start(s32[64]{0:T(128)} %param.6) | copy-start | bytes 772
  197.0 7.8 %collective-permute-start.3 = (bf16[4,64]{1,0:T(4,128)(2,1)S(1)}, bf16[4,64]{1,0:T(4,128)(2,1)S(1)}, u32[]{:S(2)}, u32[]{:S(2)}) collective-permute-start(bf16[4,64]{1,0:T(4,128)(2,1)S(1)} %convert_element_type.45), channel_id=1, source_target_pairs={{2,0},{3,1},{4,2},{5,3},{6,4},{7,5},{8,6},{9,7},{10,8},{11,9},{12,... | collective-permute-start | bytes 1544 | tf_op jit(solution)/shard_map/ppermute | solution.py:20
  200.8 5.2 %collective-permute-start.2 = (bf16[4,64]{1,0:T(4,128)(2,1)S(1)}, bf16[4,64]{1,0:T(4,128)(2,1)S(1)}, u32[]{:S(2)}, u32[]{:S(2)}) collective-permute-start(bf16[4,64]{1,0:T(4,128)(2,1)S(1)} %convert_element_type.45), channel_id=1, source_target_pairs={{1,0},{2,1},{3,2},{4,3},{5,4},{6,5},{7,6},{8,7},{9,8},{10,9},{11,1... | collective-permute-start | bytes 1544 | tf_op jit(solution)/shard_map/ppermute | solution.py:20
Sparse Core Ops, SparseCore 0:
  197.1 57.5 all-reduce.3
where the time goes:
time: 265 us; the launch traced here: 264 us
  other arithmetic  100 us (38%)
  local copies, waits for them, and re-layouts  54.9 us (21%)
  waiting for transfers between devices  52.7 us (20%)
  starting transfers between devices  33.6 us (13%)
  between operations  13.7 us (5%)
  matrix products  9.39 us (4%)
    another operation x2, other arithmetic  53.2 us
    psum x1, waiting for transfers between devices, local(): lax.psum(lag_band(block_full, KH).astype(jnp.bfloat16), 'grp')  48 us
    unnamed x1, other arithmetic  45.2 us
    unnamed x10, local copies, waits for them, and re-layouts  25.6 us
    all_to_all x1, starting transfers between devices, local(): lax.all_to_all(raw_strain, 'ch', split_axis=2, concat_axis=1, tiled=True)  19.7 us
    all_to_all x3, local copies, waits for them, and re-layouts, local(): lax.all_to_all(raw_strain, 'ch', split_axis=2, concat_axis=1, tiled=True)  16.6 us
    ppermute x4, starting transfers between devices, from_behind(): return lax.ppermute(array, axis, pairs)  13.7 us
    dot_general x1, matrix products, local(): jnp.einsum('nta,tf->naf', lax.all_to_all(raw_strain, 'ch', split_axis=2,...  5.6 us
  transfers between devices with their start and end apart: 6, of which 5 were waited for; matrix products, arithmetic and copies ran while one was open for 19% of the time, Pallas kernels for 0%

commit v1 on v0

v1 whole, which is shorter than its diff:
```python
import jax
import jax.numpy as jnp
from jax import lax
from jax.sharding import PartitionSpec as P

NT = 7680
F = 384
KH = 128
SMOOTH = 65
LAGS = 32
LAG_STEP = 10


eps_white = 1e-06


def from_behind(array, axis, by):
    count = lax.axis_size(axis)
    pairs = [(i, i + by) for i in range(count) if 0 <= i + by < count]
    return lax.ppermute(array, axis, pairs)


def smoothing_matrix(bin_count, window_bins):
    row_index = jnp.arange(bin_count, dtype=jnp.int32)[:, None]
    col_index = jnp.arange(bin_count, dtype=jnp.int32)[None, :]
    distance = (row_index - col_index) % bin_count
    halfwidth = window_bins // 2
    inside = (distance <= halfwidth) | (distance >= bin_count - halfwidth)
    return inside.astype(jnp.float32)


def whiten(spectra, bin_count, window_bins):
    real_part = spectra[..., :bin_count]
    imag_part = spectra[..., bin_count:]
    magnitude = jnp.sqrt(real_part * real_part + imag_part * imag_part)
    averaged = (
        jnp.dot(
            magnitude,
            smoothing_matrix(bin_count, window_bins),
            precision=lax.Precision.HIGHEST,
            preferred_element_type=jnp.float32,
        )
        / window_bins
    )
    factor = 1.0 / (averaged + eps_white)
    return (spectra * jnp.concatenate([factor, factor], axis=-1)).astype(jnp.bfloat16)


def phase_of(index, samples):
    return (index % samples).astype(jnp.float32) * (2.0 * jnp.pi / samples)


def dft_rows(block_starts, offsets, samples, bin_count):
    orders = jnp.arange(1, bin_count + 1, dtype=jnp.int32)[None, :]
    outer = phase_of(block_starts[:, None] * orders, samples)
    inner = phase_of(offsets[:, None] * orders, samples)
    outer_cos, outer_sin = jnp.cos(outer)[:, None, :], jnp.sin(outer)[:, None, :]
    inner_cos, inner_sin = jnp.cos(inner)[None, :, :], jnp.sin(inner)[None, :, :]
    cosine = outer_cos * inner_cos - outer_sin * inner_sin
    sine_part = outer_sin * inner_cos + outer_cos * inner_sin
    table = jnp.concatenate([cosine, -sine_part], axis=-1)
    return table.reshape(-1, 2 * bin_count).astype(jnp.bfloat16)


def unturned(own, lag_first, lag_count, lag_step, samples, bin_count):
    orders = jnp.arange(1, bin_count + 1, dtype=jnp.int32)[None, :]
    shifts = ((lag_first + jnp.arange(lag_count, dtype=jnp.int32)) * lag_step)[:, None]
    phases = (shifts * orders % samples).astype(jnp.float32) * (2.0 * jnp.pi / samples)
    cosine = jnp.cos(phases)
    sine_part = jnp.sin(phases)
    real_part = own[..., :bin_count].astype(jnp.float32)[..., None, :]
    imag_part = own[..., bin_count:].astype(jnp.float32)[..., None, :]
    back_real = real_part * cosine - imag_part * sine_part
    back_imag = imag_part * cosine + real_part * sine_part
    return jnp.concatenate([back_real, back_imag], axis=-1).astype(jnp.bfloat16)


def diagonal_band(matrix, offsets):
    row_count, col_count = matrix.shape
    flat_rows = matrix.reshape(row_count * col_count)
    padded = jnp.concatenate([flat_rows, jnp.zeros((row_count,), matrix.dtype)])
    skewed = padded.reshape(row_count, col_count + 1)
    return skewed[:, :offsets]


def lag_band(block, offsets):
    rows, lags, cols = block.shape
    flat_rows = block.reshape(rows * lags * cols)
    padded = jnp.concatenate([flat_rows, jnp.zeros((rows,), block.dtype)])
    skewed = padded.reshape(rows, lags * cols + 1)[:, : lags * cols]
    return skewed.reshape(rows, lags, cols)[:, :, :offsets]


def normalise(lagged, pair_counts, band_lows, band_highs, bin_count):
    offsets = jnp.arange(lagged.shape[2], dtype=jnp.int32)[None, :]
    in_band = (offsets >= band_lows[:, None]) & (offsets < band_highs[:, None])
    weights = jnp.where(
        in_band, 1.0 / jnp.sqrt(float(bin_count) * jnp.maximum(pair_counts, 1.0)), 0.0
    )
    return lagged * weights[:, None, :]


def local(raw_strain, window_valid, band_first, band_end):
    n_ch = lax.axis_size("ch")
    n_grp = lax.axis_size("grp")
    _, t_here, channels = raw_strain.shape
    per_dev = channels // n_ch
    pair_width = 2 * per_dev
    half = ((t_here + 1) // 2 + 15) // 16 * 16
    me = lax.axis_index("ch")
    side = me % 2

    samples = jnp.pad(raw_strain[0], ((0, 2 * half - t_here), (0, 0)))
    samples = samples.reshape(2, half, n_ch // 2, pair_width).transpose(2, 0, 1, 3)
    samples = samples.reshape(n_ch, half, pair_width)
    samples = lax.all_to_all(samples, "ch", 0, 0, tiled=True)
    samples = samples.reshape(n_ch * half, pair_width)

    block_starts = jnp.arange(n_ch, dtype=jnp.int32) * t_here
    offsets = side * half + jnp.arange(half, dtype=jnp.int32)
    table = dft_rows(block_starts, offsets, NT, F)
    partial = jnp.einsum("tc,tf->cf", samples, table, preferred_element_type=jnp.float32)
    mine = lax.dynamic_slice_in_dim(partial, side * per_dev, per_dev, 0)
    theirs = lax.dynamic_slice_in_dim(partial, (1 - side) * per_dev, per_dev, 0)
    theirs = lax.ppermute(theirs, "ch", [(j, j ^ 1) for j in range(n_ch)])
    spectra = mine + theirs

    whitened = whiten(spectra, F, SMOOTH)
    valid_flags = window_valid.astype(jnp.bfloat16)
    group_index = lax.axis_index("grp")
    own_flags = lax.dynamic_slice_in_dim(valid_flags, group_index, 1, 0)
    whitened = whitened * own_flags[0][:, None]
    blocks_up = (KH + per_dev - 1) // per_dev
    white_parts = [whitened]
    flag_parts = [valid_flags]
    for neighbour in range(1, blocks_up + 1):
        moved_white, moved_flags = from_behind((whitened, valid_flags), "ch", -neighbour)
        white_parts.append(moved_white)
        flag_parts.append(moved_flags)
    extended = jnp.concatenate(white_parts, axis=0)
    ext_flags = jnp.concatenate(flag_parts, axis=1)

    windows = [extended]
    for shift in range(1, n_grp):
        pairs = [(g, (g - shift) % n_grp) for g in range(n_grp)]
        windows.append(lax.ppermute(extended, "grp", pairs))
    windows = jnp.stack(windows)

    pair_full = jnp.einsum("na,nb->ab", valid_flags, ext_flags, preferred_element_type=jnp.float32)
    pair_counts = diagonal_band(pair_full, KH)
    turned = unturned(windows[:, :per_dev], -(LAGS // 2), LAGS, LAG_STEP, NT, F)
    block = jnp.einsum("walj,wbj->alb", turned, windows, preferred_element_type=jnp.float32)
    lagged = lag_band(block, KH)
    return normalise(lagged, pair_counts, band_first, band_end, F)


def solution(mesh):
    placed = (P("grp", "ch", None), P(None, "ch"), P("ch"), P("ch"))
    return jax.shard_map(
        local, mesh=mesh, in_specs=placed, out_specs=P("ch", None, None), check_vma=False
    )
```

time: 265 us -> 138 us (0.52)
  the two profiles are of different devices: /device:TPU:16 before, /device:TPU:10 now
where the time goes in v1:
time: 138 us; the launch traced here: 137 us
  waiting for transfers between devices  61.4 us (44%)
  starting transfers between devices  43.5 us (32%)
  other arithmetic  11.7 us (8%)
  matrix products  10.2 us (7%)
  local copies, waits for them, and re-layouts  10.1 us (7%)
    all_to_all x1, waiting for transfers between devices, local(): samples = lax.all_to_all(samples, 'ch', 0, 0, tiled=True)  49.8 us
    all_to_all x1, starting transfers between devices, local(): samples = lax.all_to_all(samples, 'ch', 0, 0, tiled=True)  20.1 us
    ppermute x4, starting transfers between devices, from_behind(): return lax.ppermute(array, axis, pairs)  11.4 us
    ppermute x3, waiting for transfers between devices, local(): windows.append(lax.ppermute(extended, 'grp', pairs))  10.3 us
    ppermute x3, starting transfers between devices, local(): windows.append(lax.ppermute(extended, 'grp', pairs))  10.1 us
    another operation x2, other arithmetic  6.92 us
    dot_general x1, matrix products, local(): jnp.einsum('walj,wbj->alb', turned, windows, preferred_element_type=jnp.f...  4.79 us
    dot_general x1, matrix products, local(): jnp.einsum('tc,tf->cf', samples, table, preferred_element_type=jnp.float32)  4.52 us
  transfers between devices with their start and end apart: 9, of which 5 were waited for; matrix products, arithmetic and copies ran while one was open for 5% of the time, Pallas kernels for 0%

profile of v1, /device:TPU:10, one launch (start us, length us, event | category | flops | bytes accessed | tf_op | source)
XLA Modules:
  0.0 137.2 jit_solution(17384715709470162123)
XLA Ops:
  0.0 1.3 pad_bitcast_fusion
  1.3 0.3 copy.13
  1.6 0.1 bitcast_bitcast_fusion
  1.7 1.6 %copy.9 = bf16[64,2,32,128]{3,2,1,0:T(8,128)(2,1)} copy(bf16[64,2,32,128]{3,0,2,1:T(8,128)(2,1)S(1)} %bitcast_bitcast_fusion) | data formatting | bytes 2097152 | tf_op jit(solution)/shard_map/transpose | solution.py:114
  3.3 20.1 %all-to-all-start = ((bf16[128,32,128]{2,1,0:T(8,128)(2,1)}), bf16[128,32,128]{2,1,0:T(8,128)(2,1)}, u32[]{:S(2)}, u32[]{:S(2)}) async-start(bf16[128,32,128]{2,1,0:T(8,128)(2,1)} %bitcast.2), calls=%async_computation | async-start | bytes 2097152 | tf_op jit(solution)/shard_map/all_to_all | solution.py:116
  23.4 1.1 fusion.44
  24.5 0.9 fusion.31
  25.4 3.5 %subtract_convert_fusion.1 = (bf16[128,32,384]{2,1,0:T(8,128)(2,1)S(1)}, bf16[128,32,384]{2,1,0:T(8,128)(2,1)}) fusion(f32[32,384]{1,0:T(8,128)S(1)} %get-tuple-element.19, f32[128,384]{1,0:T(8,128)S(1)} %get-tuple-element.16, f32[32,384]{1,0:T(8,128)S(1)} %get-tuple-element.20, f32[128,384]{1,0:T(8,128)S(1)} %get-tuple-element.15), kind=kLoop, calls=%fused_computation.11 | loop fusion | flops 14155776 | bytes 6782976 | tf_op jit(solution)/shard_map/convert.5
  29.0 0.0 copy-start.2
  29.0 49.8 %all-to-all-done = bf16[128,32,128]{2,1,0:T(8,128)(2,1)} async-done(((bf16[128,32,128]{2,1,0:T(8,128)(2,1)}), bf16[128,32,128]{2,1,0:T(8,128)(2,1)}, u32[]{:S(2)}, u32[]{:S(2)}) %all-to-all-start) | async-done | bytes 1048608 | tf_op jit(solution)/shard_map/all_to_all | solution.py:116
  78.7 0.0 copy-start.3
  78.7 0.0 copy-start.4
  78.7 4.5 %fusion.4 = f32[128,768]{1,0:T(8,128)S(1)} fusion(bf16[4096,128]{1,0:T(8,128)(2,1)} %bitcast.3, bf16[4096,384]{1,0:T(8,128)(2,1)} %bitcast.32, bf16[4096,384]{1,0:T(8,128)(2,1)S(1)} %bitcast.31), kind=kOutput, calls=%fused_computation.6 | convolution fusion | flops 817889280 | bytes 7733248 | tf_op jit(solution)/shard_map/tc,tf->cf/dot_general | solution.py:122
  83.2 0.0 copy-start
  83.3 0.0 copy-start.1
  83.3 1.9 %collective-permute-start = (f32[64,768]{1,0:T(8,128)S(1)}, f32[64,768]{1,0:T(8,128)S(1)}, u32[]{:S(2)}, u32[]{:S(2)}) collective-permute-start(f32[64,768]{1,0:T(8,128)S(1)} %constant_dynamic-slice_fusion.1), channel_id=1, source_target_pairs={{0,1},{1,0},{2,3},{3,2},{4,5},{5,4},{6,7},{7,6},{8,9},{9,8},{10,11... | collective-permute-start | bytes 589832 | tf_op jit(solution)/shard_map/ppermute | solution.py:125
  85.2 0.0 copy-done.2
  85.3 1.4 collective-permute-done
  86.7 0.7 fusion.13
  87.3 0.1 fusion.33
  87.4 1.9 %collective-permute-start.1 = (bf16[64,768]{1,0:T(8,128)(2,1)S(1)}, bf16[64,768]{1,0:T(8,128)(2,1)S(1)}, u32[]{:S(2)}, u32[]{:S(2)}) collective-permute-start(bf16[64,768]{1,0:T(8,128)(2,1)S(1)} %fusion.33), channel_id=1, source_target_pairs={{1,0},{2,1},{3,2},{4,3},{5,4},{6,5},{7,6},{8,7},{9,8},{10,9},{11,1... | collective-permute-start | bytes 294920 | tf_op jit(solution)/shard_map/ppermute | solution.py:20
  89.4 5.0 %collective-permute-start.2 = (bf16[64,768]{1,0:T(8,128)(2,1)S(1)}, bf16[64,768]{1,0:T(8,128)(2,1)S(1)}, u32[]{:S(2)}, u32[]{:S(2)}) collective-permute-start(bf16[64,768]{1,0:T(8,128)(2,1)S(1)} %fusion.33), channel_id=1, source_target_pairs={{2,0},{3,1},{4,2},{5,3},{6,4},{7,5},{8,6},{9,7},{10,8},{11,9},{12,... | collective-permute-start | bytes 294920 | tf_op jit(solution)/shard_map/ppermute | solution.py:20
  94.4 2.0 %collective-permute-start.6 = (bf16[4,64]{1,0:T(4,128)(2,1)S(1)}, bf16[4,64]{1,0:T(4,128)(2,1)S(1)}, u32[]{:S(2)}, u32[]{:S(2)}) collective-permute-start(bf16[4,64]{1,0:T(4,128)(2,1)S(1)} %convert_element_type.62), channel_id=1, source_target_pairs={{1,0},{2,1},{3,2},{4,3},{5,4},{6,5},{7,6},{8,7},{9,8},{10,9},{11,1... | collective-permute-start | bytes 1544 | tf_op jit(solution)/shard_map/ppermute | solution.py:20
  96.4 2.5 %collective-permute-start.7 = (bf16[4,64]{1,0:T(4,128)(2,1)S(1)}, bf16[4,64]{1,0:T(4,128)(2,1)S(1)}, u32[]{:S(2)}, u32[]{:S(2)}) collective-permute-start(bf16[4,64]{1,0:T(4,128)(2,1)S(1)} %convert_element_type.62), channel_id=1, source_target_pairs={{2,0},{3,1},{4,2},{5,3},{6,4},{7,5},{8,6},{9,7},{10,8},{11,9},{12,... | collective-permute-start | bytes 1544 | tf_op jit(solution)/shard_map/ppermute | solution.py:20
  98.9 0.0 collective-permute-done.1
  98.9 0.0 collective-permute-done.2
  99.0 3.4 %collective-permute-start.5 = (bf16[192,768]{1,0:T(8,128)(2,1)S(1)}, bf16[192,768]{1,0:T(8,128)(2,1)S(1)}, u32[]{:S(2)}, u32[]{:S(2)}) collective-permute-start(bf16[192,768]{1,0:T(8,128)(2,1)S(1)} %get-tuple-element.12), channel_id=1, source_target_pairs={{0,128},{128,256},{256,384},{384,0},{1,129},{129,257},{257,385},{3... | collective-permute-start | bytes 884744 | tf_op jit(solution)/shard_map/ppermute | solution.py:146
  102.4 2.4 %collective-permute-start.3 = (bf16[192,768]{1,0:T(8,128)(2,1)S(1)}, bf16[192,768]{1,0:T(8,128)(2,1)S(1)}, u32[]{:S(2)}, u32[]{:S(2)}) collective-permute-start(bf16[192,768]{1,0:T(8,128)(2,1)S(1)} %get-tuple-element.12), channel_id=1, source_target_pairs={{0,384},{128,0},{256,128},{384,256},{1,385},{129,1},{257,129},{385... | collective-permute-start | bytes 884744 | tf_op jit(solution)/shard_map/ppermute | solution.py:146
  104.8 4.2 %collective-permute-start.4 = (bf16[192,768]{1,0:T(8,128)(2,1)S(1)}, bf16[192,768]{1,0:T(8,128)(2,1)S(1)}, u32[]{:S(2)}, u32[]{:S(2)}) collective-permute-start(bf16[192,768]{1,0:T(8,128)(2,1)S(1)} %get-tuple-element.12), channel_id=1, source_target_pairs={{0,256},{128,384},{256,0},{384,128},{1,257},{129,385},{257,1},{385... | collective-permute-start | bytes 884744 | tf_op jit(solution)/shard_map/ppermute | solution.py:146
  109.0 0.0 collective-permute-done.6
  109.1 0.0 collective-permute-done.7
  109.1 0.2 convolution_bitcast_fusion
  109.3 0.1 reshape.254
  109.4 0.2 reshape.255
  109.6 0.0 copy-done.3
  109.6 0.0 copy-done.4
  109.6 0.1 fusion.53
  109.7 0.2 collective-permute-done.5
  109.9 3.6 %collective-permute-done.3 = bf16[192,768]{1,0:T(8,128)(2,1)S(1)} collective-permute-done((bf16[192,768]{1,0:T(8,128)(2,1)S(1)}, bf16[192,768]{1,0:T(8,128)(2,1)S(1)}, u32[]{:S(2)}, u32[]{:S(2)}) %collective-permute-start.3) | collective-permute-done | bytes 294944 | tf_op jit(solution)/shard_map/ppermute | solution.py:146
  113.5 6.5 %collective-permute-done.4 = bf16[192,768]{1,0:T(8,128)(2,1)S(1)} collective-permute-done((bf16[192,768]{1,0:T(8,128)(2,1)S(1)}, bf16[192,768]{1,0:T(8,128)(2,1)S(1)}, u32[]{:S(2)}, u32[]{:S(2)}) %collective-permute-start.4) | collective-permute-done | bytes 294944 | tf_op jit(solution)/shard_map/ppermute | solution.py:146
  120.0 0.1 pad_maximum_fusion
  120.1 0.1 slice_convert_fusion.1
  120.2 0.3 copy.10
  120.5 0.3 copy.11
  120.7 0.0 copy-done
  120.7 0.0 copy-done.1
  120.8 3.4 %subtract_convert_fusion = (bf16[4,64,32,384]{3,2,0,1:T(8,128)(2,1)S(1)}, bf16[4,64,32,384]{3,2,0,1:T(8,128)(2,1)S(1)}) fusion(f32[32,384]{1,0:T(8,128)S(1)} %copy-done.1, f32[4,64,384]{2,0,1:T(4,128)S(1)} %copy.11, f32[32,384]{1,0:T(8,128)S(1)} %copy-done, f32[4,64,384]{2,0,1:T(4,128)S(1)} %copy.10), kind=kLoop, calls=%fused_computation.5 | loop fusion | flops 25165824 | bytes 13467648 | tf_op jit(solution)/shard_map/convert
  124.1 4.8 %fusion.8 = f32[64,32,192]{2,1,0:T(8,128)} fusion(bf16[4,64,32,384]{3,2,0,1:T(8,128)(2,1)S(1)} %get-tuple-element.8, bf16[4,64,32,384]{3,2,0,1:T(8,128)(2,1)S(1)} %get-tuple-element.7, bf16[1,192,768]{2,1,0:T(8,128)(2,1)S(1)} %bitcast.35, bf16[1,192,768]{2,1,0:T(8,128)(2,1)S(1)} %bitcast.39, bf16[1,192,768]{2,1,0:T(8,128)(2,1)S(1)} %bitcast.37, ...), kind=kOutput, calls=%fused_computation.12 | convolution fusion | flops 2442854400 | bytes 15335424 | tf_op jit(solution)/shard_map/walj,wbj->alb/dot_general | solution.py:152
  128.9 2.4 %reshape.251 = f32[393216]{0:T(1024)S(1)} reshape(f32[64,32,192]{2,1,0:T(8,128)} %fusion.8) | data formatting | bytes 3145728 | tf_op jit(solution)/shard_map/reshape | solution.py:88
  131.3 0.1 concatenate.28
  131.5 1.0 reshape.252
  132.5 0.1 slice.35
  132.6 2.3 %reshape.253 = f32[64,32,192]{2,1,0:T(8,128)} reshape(f32[64,6144]{1,0:T(8,128)S(1)} %slice.35) | data formatting | bytes 3145728 | tf_op jit(solution)/shard_map/reshape | solution.py:91
  134.9 2.3 %slice_multiply_fusion = f32[64,32,128]{2,1,0:T(8,128)} fusion(f32[64,32,192]{2,1,0:T(8,128)} %reshape.253, f32[64,128]{1,0:T(8,128)S(1)} %fusion.53), kind=kLoop, calls=%fused_computation.20 | loop fusion | flops 262144 | bytes 2129920 | tf_op jit(solution)/shard_map/mul | solution.py:100
  (9 shorter events, 0.1 us)
Async XLA Ops:
  3.3 75.4 %all-to-all-start = ((bf16[128,32,128]{2,1,0:T(8,128)(2,1)}), bf16[128,32,128]{2,1,0:T(8,128)(2,1)}, u32[]{:S(2)}, u32[]{:S(2)}) async-start(bf16[128,32,128]{2,1,0:T(8,128)(2,1)} %bitcast.2), calls=%async_computation | async-start | bytes 2097152 | tf_op jit(solution)/shard_map/all_to_all | solution.py:116
  29.0 56.3 %copy-start.2 = (s32[4,64]{1,0:T(4,128)S(1)}, s32[4,64]{1,0:T(4,128)}, u32[]{:S(2)}) copy-start(s32[4,64]{1,0:T(4,128)} %param.5) | copy-start | bytes 3076
  78.7 30.9 %copy-start.3 = (s32[64]{0:T(128)S(1)}, s32[64]{0:T(128)}, u32[]{:S(2)}) copy-start(s32[64]{0:T(128)} %param.7) | copy-start | bytes 772
  78.7 30.9 %copy-start.4 = (s32[64]{0:T(128)S(1)}, s32[64]{0:T(128)}, u32[]{:S(2)}) copy-start(s32[64]{0:T(128)} %param.6) | copy-start | bytes 772
  83.2 37.5 %copy-start = (f32[32,384]{1,0:T(8,128)S(1)}, f32[32,384]{1,0:T(8,128)}, u32[]{:S(2)}) copy-start(f32[32,384]{1,0:T(8,128)} %get-tuple-element.13) | copy-start | bytes 147460
  83.3 37.5 %copy-start.1 = (f32[32,384]{1,0:T(8,128)S(1)}, f32[32,384]{1,0:T(8,128)}, u32[]{:S(2)}) copy-start(f32[32,384]{1,0:T(8,128)} %get-tuple-element.14) | copy-start | bytes 147460
  83.3 3.3 %collective-permute-start = (f32[64,768]{1,0:T(8,128)S(1)}, f32[64,768]{1,0:T(8,128)S(1)}, u32[]{:S(2)}, u32[]{:S(2)}) collective-permute-start(f32[64,768]{1,0:T(8,128)S(1)} %constant_dynamic-slice_fusion.1), channel_id=1, source_target_pairs={{0,1},{1,0},{2,3},{3,2},{4,5},{5,4},{6,7},{7,6},{8,9},{9,8},{10,11... | collective-permute-start | bytes 589832 | tf_op jit(solution)/shard_map/ppermute | solution.py:125
  87.4 11.5 %collective-permute-start.1 = (bf16[64,768]{1,0:T(8,128)(2,1)S(1)}, bf16[64,768]{1,0:T(8,128)(2,1)S(1)}, u32[]{:S(2)}, u32[]{:S(2)}) collective-permute-start(bf16[64,768]{1,0:T(8,128)(2,1)S(1)} %fusion.33), channel_id=1, source_target_pairs={{1,0},{2,1},{3,2},{4,3},{5,4},{6,5},{7,6},{8,7},{9,8},{10,9},{11,1... | collective-permute-start | bytes 294920 | tf_op jit(solution)/shard_map/ppermute | solution.py:20
  89.4 9.5 %collective-permute-start.2 = (bf16[64,768]{1,0:T(8,128)(2,1)S(1)}, bf16[64,768]{1,0:T(8,128)(2,1)S(1)}, u32[]{:S(2)}, u32[]{:S(2)}) collective-permute-start(bf16[64,768]{1,0:T(8,128)(2,1)S(1)} %fusion.33), channel_id=1, source_target_pairs={{2,0},{3,1},{4,2},{5,3},{6,4},{7,5},{8,6},{9,7},{10,8},{11,9},{12,... | collective-permute-start | bytes 294920 | tf_op jit(solution)/shard_map/ppermute | solution.py:20
  94.4 14.7 %collective-permute-start.6 = (bf16[4,64]{1,0:T(4,128)(2,1)S(1)}, bf16[4,64]{1,0:T(4,128)(2,1)S(1)}, u32[]{:S(2)}, u32[]{:S(2)}) collective-permute-start(bf16[4,64]{1,0:T(4,128)(2,1)S(1)} %convert_element_type.62), channel_id=1, source_target_pairs={{1,0},{2,1},{3,2},{4,3},{5,4},{6,5},{7,6},{8,7},{9,8},{10,9},{11,1... | collective-permute-start | bytes 1544 | tf_op jit(solution)/shard_map/ppermute | solution.py:20
  96.4 12.7 %collective-permute-start.7 = (bf16[4,64]{1,0:T(4,128)(2,1)S(1)}, bf16[4,64]{1,0:T(4,128)(2,1)S(1)}, u32[]{:S(2)}, u32[]{:S(2)}) collective-permute-start(bf16[4,64]{1,0:T(4,128)(2,1)S(1)} %convert_element_type.62), channel_id=1, source_target_pairs={{2,0},{3,1},{4,2},{5,3},{6,4},{7,5},{8,6},{9,7},{10,8},{11,9},{12,... | collective-permute-start | bytes 1544 | tf_op jit(solution)/shard_map/ppermute | solution.py:20
  99.0 11.0 %collective-permute-start.5 = (bf16[192,768]{1,0:T(8,128)(2,1)S(1)}, bf16[192,768]{1,0:T(8,128)(2,1)S(1)}, u32[]{:S(2)}, u32[]{:S(2)}) collective-permute-start(bf16[192,768]{1,0:T(8,128)(2,1)S(1)} %get-tuple-element.12), channel_id=1, source_target_pairs={{0,128},{128,256},{256,384},{384,0},{1,129},{129,257},{257,385},{3... | collective-permute-start | bytes 884744 | tf_op jit(solution)/shard_map/ppermute | solution.py:146
  102.4 11.1 %collective-permute-start.3 = (bf16[192,768]{1,0:T(8,128)(2,1)S(1)}, bf16[192,768]{1,0:T(8,128)(2,1)S(1)}, u32[]{:S(2)}, u32[]{:S(2)}) collective-permute-start(bf16[192,768]{1,0:T(8,128)(2,1)S(1)} %get-tuple-element.12), channel_id=1, source_target_pairs={{0,384},{128,0},{256,128},{384,256},{1,385},{129,1},{257,129},{385... | collective-permute-start | bytes 884744 | tf_op jit(solution)/shard_map/ppermute | solution.py:146
  104.8 15.2 %collective-permute-start.4 = (bf16[192,768]{1,0:T(8,128)(2,1)S(1)}, bf16[192,768]{1,0:T(8,128)(2,1)S(1)}, u32[]{:S(2)}, u32[]{:S(2)}) collective-permute-start(bf16[192,768]{1,0:T(8,128)(2,1)S(1)} %get-tuple-element.12), channel_id=1, source_target_pairs={{0,256},{128,384},{256,0},{384,128},{1,257},{129,385},{257,1},{385... | collective-permute-start | bytes 884744 | tf_op jit(solution)/shard_map/ppermute | solution.py:146
